TPU v7x, 512 devices: a whole 4x8x8 slice. The times are simulated.
512 devices in a mesh: chan: 32 (over y_hi, x, core), tm: 16 (over y_lo, z).
Axes of the slice: x: 4, y: 8 (y_hi: 4, y_lo: 2; y = y_hi * 2 + y_lo), z: 8, core: 2. Of those that a mesh axis runs over, the one named last changes fastest.
Arguments:
- raw_strain: float32 [2048, 16384], P('chan', 'tm'), may hold values from -2000 to 2000
- fir_taps: float32 [64], replicated, may hold values from -0.75 to 0.75
- block_mask: int32 [32, 32], replicated, may hold values 0 or 1
Outputs:
- correlations: float32 [128, 2048, 2048], P('tm', 'chan')
All inputs are finite; a program needn't handle non-finite values.
Results may differ from a plain program's by a relative error of at most 0.0054.
Values may be sent and summed in bfloat16 or wider, within the bound.
No kernel may reach another device: no remote copies, remote signals or barrier semaphores. Data moves between devices by JAX's collectives and lax.ppermute only.
A program may use at most 64 MiB of HBM per device.

v0:
```python
import math
import jax
import jax.numpy as jnp
from jax import lax
from jax.sharding import PartitionSpec as P

DECIM = 8
TAPS = 64
LAGS = 128


def from_behind(value, axis, steps):
    count = lax.axis_size(axis)
    first, last = (max(0, -steps), min(count, count - steps))
    return lax.ppermute(value, axis, [(source, source + steps) for source in range(first, last)])


def decimate(raw_strain, fir_taps):
    time_span = raw_strain.shape[1]
    margin = TAPS - DECIM
    earlier = from_behind(raw_strain[:, time_span - margin :], "tm", 1)
    extended = jnp.concatenate([earlier, raw_strain], axis=1)
    outputs = time_span // DECIM
    tap_blocks = TAPS // DECIM
    frames = outputs + tap_blocks - 1
    tap_table = fir_taps[::-1].reshape(tap_blocks, DECIM)
    shape_three = (frames, outputs, tap_blocks)
    matches = lax.broadcasted_iota(jnp.int32, shape_three, 0) - lax.broadcasted_iota(
        jnp.int32, shape_three, 1
    ) == lax.broadcasted_iota(jnp.int32, shape_three, 2)
    one_hot = matches.astype(jnp.float32)
    filter_matrix = jnp.einsum("mtj,jr->mrt", one_hot, tap_table, precision=lax.Precision.HIGHEST)
    filter_matrix = filter_matrix.reshape(frames * DECIM, outputs)
    return jnp.dot(
        extended, filter_matrix, precision=lax.Precision.HIGHEST, preferred_element_type=jnp.float32
    )


def per_device(raw_strain, fir_taps, block_mask):
    channel_rows = raw_strain.shape[0]
    decimated = decimate(raw_strain, fir_taps)
    rounded = decimated.astype(jnp.bfloat16)
    time_span = rounded.shape[1]
    tm_parts = lax.axis_size("tm")
    samples = time_span * tm_parts
    gathered = lax.all_gather(rounded, "tm", axis=1, tiled=True)
    full_values = gathered.astype(jnp.float32)
    root_whole = jnp.sqrt(jnp.mean(full_values * full_values, axis=1, keepdims=True) + 1e-06)
    caches = (full_values / root_whole).astype(jnp.bfloat16)
    lag_count = LAGS // tm_parts
    tm_index = lax.axis_index("tm")
    lag_base = tm_index * lag_count
    anchor = jnp.zeros((), jnp.int32)
    initial = jnp.zeros(
        (lag_count, channel_rows, channel_rows * lax.axis_size("chan")), jnp.float32
    )
    shard_piece = lax.all_gather(caches, "chan", axis=0, tiled=True)
    first_index = jnp.int32(0)
    piece_width = shard_piece.shape[0]
    padded_piece = jnp.pad(shard_piece, ((0, 0), (0, LAGS)))

    def one_lag(lag_step, running):
        shifted = lax.dynamic_slice_in_dim(padded_piece, lag_base + lag_step, samples, 1)
        product = lax.dot_general(
            caches, shifted, (((1,), (1,)), ((), ())), preferred_element_type=jnp.float32
        )
        where_at = (lag_step, anchor, first_index)
        current = lax.dynamic_slice(running, where_at, (1, channel_rows, piece_width))
        return lax.dynamic_update_slice(running, current + product[None], where_at)

    correlated = lax.fori_loop(0, lag_count, one_lag, initial)
    mask_row = lax.dynamic_index_in_dim(block_mask, lax.axis_index("chan"), 0, keepdims=False)
    weights = jnp.repeat(mask_row, channel_rows).astype(jnp.float32) * (1.0 / math.sqrt(samples))
    return correlated * weights[None, None, :]


def solution(mesh):
    placed = (P("chan", "tm"), P(), P())
    return jax.shard_map(
        per_device, mesh=mesh, in_specs=placed, out_specs=P("tm", "chan", None), check_vma=False
    )
```

profile of v0, /device:TPU:17, one launch (start us, length us, event | category | flops | bytes accessed | tf_op | source)
XLA Modules:
  0.0 219.1 jit_solution(5011104009306333967)
XLA Ops:
  6.5 0.0 all-gather.2.cloned.1.call-start
  6.5 0.8 slice.3
  7.4 4.0 %collective-permute-start = (f32[64,56]{1,0:T(8,128)S(1)}, f32[64,56]{1,0:T(8,128)S(1)}, u32[]{:S(2)}, u32[]{:S(2)}) collective-permute-start(f32[64,56]{1,0:T(8,128)S(1)} %slice.3), channel_id=1, source_target_pairs={{0,1},{1,2},{2,3},{3,4},{4,5},{5,6},{6,7},{7,8},{8,9},{9,10},{10,1... | collective-permute-start | bytes 43016 | tf_op jit(solution)/shard_map/ppermute | solution.py:15
  11.4 0.7 rev.3
  12.1 0.1 reshape.27
  12.2 0.4 convolution_bitcast_fusion
  12.6 0.0 collective-permute-done
  12.7 1.5 convolution_convert_fusion
  14.1 33.4 %all_gather.6 = bf16[64,2048]{1,0:T(8,128)(2,1)S(1)} all-gather(bf16[64,128]{1,0:T(8,128)(2,1)S(1)} %convolution_convert_fusion), channel_id=1, replica_groups=mesh['chan'=32,'tm'=16] {'tm'}, dimensions={1}, use_global_device_ids=true | all-gather | bytes 278528 | tf_op jit(solution)/shard_map/all_gather | solution.py:46
  47.5 0.2 fusion.12
  47.7 0.8 fusion.13
  48.5 0.0 all-gather.2.cloned.1.call-update
  48.6 0.7 multiply_bitcast_fusion
  49.3 0.1 broadcast_in_dim.16
  49.3 0.1 mul.36
  49.4 86.4 %all-gather.2.cloned.1.call-done = bf16[2048,2048]{1,0:T(8,128)(2,1)} async-done(((bf16[64,2048]{1,0:T(8,128)(2,1)}), bf16[2048,2048]{1,0:T(8,128)(2,1)}) %all-gather.2.cloned.1.call-update) | async-done | bytes 8388624 | tf_op jit(solution)/shard_map/all_gather | solution.py:57
  135.8 7.8 %pad.4 = bf16[2048,2176]{1,0:T(8,128)(2,1)} pad(bf16[2048,2048]{1,0:T(8,128)(2,1)} %all-gather.2.cloned.1.call-done, bf16[]{:T(256)} %constant.53.clone.1), padding=0_0x0_128 | pad | bytes 17301506 | tf_op jit(solution)/shard_map/jit(_pad)/pad | solution.py:60
  143.6 0.0 copy-start
  143.6 2.5 %broadcast_in_dim.15 = f32[8,64,2048]{2,1,0:T(8,128)} broadcast(f32[]{:T(128)} %constant.48.clone.1), dimensions={} | broadcast | bytes 4194308 | tf_op jit(solution)/shard_map/broadcast_in_dim | solution.py:54
  146.1 0.0 copy-done
  146.1 61.2 %while.13 = (s32[]{:T(128)}, f32[8,64,2048]{2,1,0:T(8,128)}, s32[]{:T(128)}, bf16[2048,2176]{1,0:T(8,128)(2,1)}, bf16[64,2048]{1,0:T(8,128)(2,1)S(1)}, /*index=5*/s32[]{:T(128)}, s32[]{:T(128)}, s32[]{:T(128)}) while((s32[]{:T(128)}, f32[8,64,2048]{2,1,0:T(8,128)}, s32[]{:T(128)}, bf16[2048,2176]{1,0:T(8,128)(2,1)}, ...), condition=%wide.region_2.3_spmd, body=%wide.region_1.2_spmd.sunk | while | flops 537001984 | bytes 9699475 | solution.py:71
  146.1 7.7 %fusion.26 = f32[8,64,2048]{2,1,0:T(8,128)} fusion(f32[8,64,2048]{2,1,0:T(8,128)} %get-tuple-element.150, s32[]{:T(128)S(6)} %copy.10, bf16[64,2048]{1,0:T(8,128)(2,1)S(1)} %get-tuple-element.161, bf16[2048,2176]{1,0:T(8,128)(2,1)} %get-tuple-element.160, s32[]{:T(128)S(6)} %select_n.19), kind=kOutput, calls=%fused_computation.4.clone.1 | convolution fusion | flops 537001984 | bytes 9699336 | tf_op jit(solution)/shard_map/while/body/eval_jaxpr/dot_general | solution.py:64
  153.8 7.7 %fusion.26 = f32[8,64,2048]{2,1,0:T(8,128)} fusion(f32[8,64,2048]{2,1,0:T(8,128)} %get-tuple-element.150, s32[]{:T(128)S(6)} %copy.10, bf16[64,2048]{1,0:T(8,128)(2,1)S(1)} %get-tuple-element.161, bf16[2048,2176]{1,0:T(8,128)(2,1)} %get-tuple-element.160, s32[]{:T(128)S(6)} %select_n.19), kind=kOutput, calls=%fused_computation.4.clone.1 | convolution fusion | flops 537001984 | bytes 9699336 | tf_op jit(solution)/shard_map/while/body/eval_jaxpr/dot_general | solution.py:64
  161.4 7.7 %fusion.26 = f32[8,64,2048]{2,1,0:T(8,128)} fusion(f32[8,64,2048]{2,1,0:T(8,128)} %get-tuple-element.150, s32[]{:T(128)S(6)} %copy.10, bf16[64,2048]{1,0:T(8,128)(2,1)S(1)} %get-tuple-element.161, bf16[2048,2176]{1,0:T(8,128)(2,1)} %get-tuple-element.160, s32[]{:T(128)S(6)} %select_n.19), kind=kOutput, calls=%fused_computation.4.clone.1 | convolution fusion | flops 537001984 | bytes 9699336 | tf_op jit(solution)/shard_map/while/body/eval_jaxpr/dot_general | solution.py:64
  169.1 7.7 %fusion.26 = f32[8,64,2048]{2,1,0:T(8,128)} fusion(f32[8,64,2048]{2,1,0:T(8,128)} %get-tuple-element.150, s32[]{:T(128)S(6)} %copy.10, bf16[64,2048]{1,0:T(8,128)(2,1)S(1)} %get-tuple-element.161, bf16[2048,2176]{1,0:T(8,128)(2,1)} %get-tuple-element.160, s32[]{:T(128)S(6)} %select_n.19), kind=kOutput, calls=%fused_computation.4.clone.1 | convolution fusion | flops 537001984 | bytes 9699336 | tf_op jit(solution)/shard_map/while/body/eval_jaxpr/dot_general | solution.py:64
  176.8 7.7 %fusion.26 = f32[8,64,2048]{2,1,0:T(8,128)} fusion(f32[8,64,2048]{2,1,0:T(8,128)} %get-tuple-element.150, s32[]{:T(128)S(6)} %copy.10, bf16[64,2048]{1,0:T(8,128)(2,1)S(1)} %get-tuple-element.161, bf16[2048,2176]{1,0:T(8,128)(2,1)} %get-tuple-element.160, s32[]{:T(128)S(6)} %select_n.19), kind=kOutput, calls=%fused_computation.4.clone.1 | convolution fusion | flops 537001984 | bytes 9699336 | tf_op jit(solution)/shard_map/while/body/eval_jaxpr/dot_general | solution.py:64
  184.4 7.7 %fusion.26 = f32[8,64,2048]{2,1,0:T(8,128)} fusion(f32[8,64,2048]{2,1,0:T(8,128)} %get-tuple-element.150, s32[]{:T(128)S(6)} %copy.10, bf16[64,2048]{1,0:T(8,128)(2,1)S(1)} %get-tuple-element.161, bf16[2048,2176]{1,0:T(8,128)(2,1)} %get-tuple-element.160, s32[]{:T(128)S(6)} %select_n.19), kind=kOutput, calls=%fused_computation.4.clone.1 | convolution fusion | flops 537001984 | bytes 9699336 | tf_op jit(solution)/shard_map/while/body/eval_jaxpr/dot_general | solution.py:64
  192.1 7.7 %fusion.26 = f32[8,64,2048]{2,1,0:T(8,128)} fusion(f32[8,64,2048]{2,1,0:T(8,128)} %get-tuple-element.150, s32[]{:T(128)S(6)} %copy.10, bf16[64,2048]{1,0:T(8,128)(2,1)S(1)} %get-tuple-element.161, bf16[2048,2176]{1,0:T(8,128)(2,1)} %get-tuple-element.160, s32[]{:T(128)S(6)} %select_n.19), kind=kOutput, calls=%fused_computation.4.clone.1 | convolution fusion | flops 537001984 | bytes 9699336 | tf_op jit(solution)/shard_map/while/body/eval_jaxpr/dot_general | solution.py:64
  199.7 7.7 %fusion.26 = f32[8,64,2048]{2,1,0:T(8,128)} fusion(f32[8,64,2048]{2,1,0:T(8,128)} %get-tuple-element.150, s32[]{:T(128)S(6)} %copy.10, bf16[64,2048]{1,0:T(8,128)(2,1)S(1)} %get-tuple-element.161, bf16[2048,2176]{1,0:T(8,128)(2,1)} %get-tuple-element.160, s32[]{:T(128)S(6)} %select_n.19), kind=kOutput, calls=%fused_computation.4.clone.1 | convolution fusion | flops 537001984 | bytes 9699336 | tf_op jit(solution)/shard_map/while/body/eval_jaxpr/dot_general | solution.py:64
  207.4 4.9 %broadcast_multiply_fusion = f32[8,64,2048]{2,1,0:T(8,128)} fusion(f32[8,64,2048]{2,1,0:T(8,128)} %get-tuple-element.99, f32[2048]{0:T(1024)S(1)} %mul.36), kind=kLoop, calls=%fused_computation.7 | loop fusion | flops 1048576 | bytes 8396800 | tf_op jit(solution)/shard_map/mul | solution.py:74
  (1 shorter events, 0.0 us)
Async XLA Ops:
  6.5 129.2 %all-gather.2.cloned.1.call-start = ((), (), s32[]{:S(2)}) async-start(), calls=%async_computation | async-start | bytes 8650752 | tf_op jit(solution)/shard_map/all_gather | solution.py:57
  7.4 5.3 %collective-permute-start = (f32[64,56]{1,0:T(8,128)S(1)}, f32[64,56]{1,0:T(8,128)S(1)}, u32[]{:S(2)}, u32[]{:S(2)}) collective-permute-start(f32[64,56]{1,0:T(8,128)S(1)} %slice.3), channel_id=1, source_target_pairs={{0,1},{1,2},{2,3},{3,4},{4,5},{5,6},{6,7},{7,8},{8,9},{9,10},{10,1... | collective-permute-start | bytes 43016 | tf_op jit(solution)/shard_map/ppermute | solution.py:15
  143.6 2.5 %copy-start = (bf16[64,2048]{1,0:T(8,128)(2,1)S(1)}, bf16[64,2048]{1,0:T(8,128)(2,1)}, u32[]{:S(2)}) copy-start(bf16[64,2048]{1,0:T(8,128)(2,1)} %fusion.13) | copy-start | bytes 786436
Sparse Core Ops, SparseCore 0:
  48.7 87.0 all-gather.1
where the time goes:
time: 219 us
  waiting for transfers between devices  86.4 us (39%)
  matrix products  63.1 us (29%)
  blocking collectives  33.4 us (15%)
  between operations  13.4 us (6%)
  local copies, waits for them, and re-layouts  12.1 us (6%)
  other arithmetic  6.58 us (3%)
  starting transfers between devices  3.99 us (2%)
    all_gather x1, waiting for transfers between devices, per_device(): shard_piece = lax.all_gather(caches, 'chan', axis=0, tiled=True)  86.4 us
    dot_general x8, matrix products, one_lag(): lax.dot_general(caches, shifted, (((1,), (1,)), ((), ())), preferred_elem...  61.2 us
    all_gather x1, blocking collectives, per_device(): gathered = lax.all_gather(rounded, 'tm', axis=1, tiled=True)  33.4 us
    pad x1, local copies, waits for them, and re-layouts, per_device(): padded_piece = jnp.pad(shard_piece, ((0, 0), (0, LAGS)))  7.82 us
    mul x1, other arithmetic, per_device(): return correlated * weights[None, None, :]  4.89 us
  transfers between devices with their start and end apart: 2, of which 1 were waited for; matrix products, arithmetic and copies ran while one was open for 1% of the time, Pallas kernels for 0%

commit v1 on v0

--- a/solution.py
+++ b/solution.py
@@ -7,6 +7,11 @@
 DECIM = 8
 TAPS = 64
 LAGS = 128
+
+
+def exchange_gather(shard, axis, dim):
+    stack = jnp.stack([shard] * lax.axis_size(axis))
+    return jnp.concatenate(lax.all_to_all(stack, axis, 0, 0), axis=dim)
 
 
 def from_behind(value, axis, steps):
@@ -43,7 +48,7 @@
     time_span = rounded.shape[1]
     tm_parts = lax.axis_size("tm")
     samples = time_span * tm_parts
-    gathered = lax.all_gather(rounded, "tm", axis=1, tiled=True)
+    gathered = exchange_gather(rounded, "tm", 1)
     full_values = gathered.astype(jnp.float32)
     root_whole = jnp.sqrt(jnp.mean(full_values * full_values, axis=1, keepdims=True) + 1e-06)
     caches = (full_values / root_whole).astype(jnp.bfloat16)

time: 219 us -> 201 us (0.918)
  blocking collectives: 33.4 us -> 19.2 us
  waiting for transfers between devices: 86.4 us -> 82.6 us
    all_gather x1 -> x0, blocking collectives: 33.4 us -> none  [per_device(): gathered = lax.all_gather(rounded, 'tm', axis=1, tiled=True)]
    all_to_all x0 -> x1, blocking collectives: none -> 19.2 us  [exchange_gather(): return jnp.concatenate(lax.all_to_all(stack, axis, 0, 0), axis=dim)]
    all_gather x1, waiting for transfers between devices: 86.4 us -> 82.6 us  [per_device(): shard_piece = lax.all_gather(caches, 'chan', axis=0, tiled=True)]
where the time goes in v1:
time: 201 us
  waiting for transfers between devices  82.6 us (41%)
  matrix products  63.1 us (31%)
  blocking collectives  19.2 us (10%)
  between operations  13.4 us (7%)
  local copies, waits for them, and re-layouts  12.2 us (6%)
  other arithmetic  6.58 us (3%)
  starting transfers between devices  3.99 us (2%)
    all_gather x1, waiting for transfers between devices, per_device(): shard_piece = lax.all_gather(caches, 'chan', axis=0, tiled=True)  82.6 us
    dot_general x8, matrix products, one_lag(): lax.dot_general(caches, shifted, (((1,), (1,)), ((), ())), preferred_elem...  61.2 us
    all_to_all x1, blocking collectives, exchange_gather(): return jnp.concatenate(lax.all_to_all(stack, axis, 0, 0), axis=dim)  19.2 us
    pad x1, local copies, waits for them, and re-layouts, per_device(): padded_piece = jnp.pad(shard_piece, ((0, 0), (0, LAGS)))  7.82 us
    mul x1, other arithmetic, per_device(): return correlated * weights[None, None, :]  4.89 us
  transfers between devices with their start and end apart: 2, of which 1 were waited for; matrix products, arithmetic and copies ran while one was open for 1% of the time, Pallas kernels for 0%

profile of v1, /device:TPU:17, one launch (start us, length us, event | category | flops | bytes accessed | tf_op | source)
XLA Modules:
  0.0 201.1 jit_solution(12012675638693323368)
XLA Ops:
  6.5 0.0 all-gather.2.cloned.1.call-start
  6.5 0.8 slice.3
  7.4 4.0 %collective-permute-start = (f32[64,56]{1,0:T(8,128)S(1)}, f32[64,56]{1,0:T(8,128)S(1)}, u32[]{:S(2)}, u32[]{:S(2)}) collective-permute-start(f32[64,56]{1,0:T(8,128)S(1)} %slice.3), channel_id=1, source_target_pairs={{0,1},{1,2},{2,3},{3,4},{4,5},{5,6},{6,7},{7,8},{8,9},{9,10},{10,1... | collective-permute-start | bytes 43016 | tf_op jit(solution)/shard_map/ppermute | solution.py:20
  11.4 0.7 rev.3
  12.1 0.1 reshape.33
  12.2 0.4 convolution_bitcast_fusion
  12.6 0.0 collective-permute-done
  12.7 1.5 convolution_convert_fusion
  14.2 19.2 %all_to_all.5 = bf16[16,64,128]{2,1,0:T(8,128)(2,1)S(1)} all-to-all(bf16[16,64,128]{2,1,0:T(8,128)(2,1)S(1)} %stack.2), channel_id=1, replica_groups=mesh['chan'=32,'tm'=16] {'tm'}, dimensions={0} | all-to-all | bytes 524288 | tf_op jit(solution)/shard_map/all_to_all | solution.py:14
  33.3 0.2 fusion.12
  33.5 0.8 fusion.13
  34.3 0.0 all-gather.2.cloned.1.call-update
  34.4 0.7 multiply_bitcast_fusion
  35.1 0.1 broadcast_in_dim.16
  35.1 0.1 mul.38
  35.2 82.6 %all-gather.2.cloned.1.call-done = bf16[2048,2048]{1,0:T(8,128)(2,1)} async-done(((bf16[64,2048]{1,0:T(8,128)(2,1)}), bf16[2048,2048]{1,0:T(8,128)(2,1)}) %all-gather.2.cloned.1.call-update) | async-done | bytes 8388624 | tf_op jit(solution)/shard_map/all_gather | solution.py:62
  117.8 7.8 %pad.4 = bf16[2048,2176]{1,0:T(8,128)(2,1)} pad(bf16[2048,2048]{1,0:T(8,128)(2,1)} %all-gather.2.cloned.1.call-done, bf16[]{:T(256)} %constant.53.clone.1), padding=0_0x0_128 | pad | bytes 17301506 | tf_op jit(solution)/shard_map/jit(_pad)/pad | solution.py:65
  125.6 0.0 copy-start
  125.6 2.5 %broadcast_in_dim.15 = f32[8,64,2048]{2,1,0:T(8,128)} broadcast(f32[]{:T(128)} %constant.48.clone.1), dimensions={} | broadcast | bytes 4194308 | tf_op jit(solution)/shard_map/broadcast_in_dim | solution.py:59
  128.2 0.0 copy-done
  128.2 61.2 %while.13 = (s32[]{:T(128)}, f32[8,64,2048]{2,1,0:T(8,128)}, s32[]{:T(128)}, bf16[2048,2176]{1,0:T(8,128)(2,1)}, bf16[64,2048]{1,0:T(8,128)(2,1)S(1)}, /*index=5*/s32[]{:T(128)}, s32[]{:T(128)}, s32[]{:T(128)}) while((s32[]{:T(128)}, f32[8,64,2048]{2,1,0:T(8,128)}, s32[]{:T(128)}, bf16[2048,2176]{1,0:T(8,128)(2,1)}, ...), condition=%wide.region_2.3_spmd, body=%wide.region_1.2_spmd.sunk | while | flops 537001984 | bytes 9699475 | solution.py:76
  128.2 7.7 %fusion.26 = f32[8,64,2048]{2,1,0:T(8,128)} fusion(f32[8,64,2048]{2,1,0:T(8,128)} %get-tuple-element.150, s32[]{:T(128)S(6)} %copy.15, bf16[64,2048]{1,0:T(8,128)(2,1)S(1)} %get-tuple-element.161, bf16[2048,2176]{1,0:T(8,128)(2,1)} %get-tuple-element.160, s32[]{:T(128)S(6)} %select_n.19), kind=kOutput, calls=%fused_computation.4.clone.1 | convolution fusion | flops 537001984 | bytes 9699336 | tf_op jit(solution)/shard_map/while/body/eval_jaxpr/dot_general | solution.py:69
  135.8 7.7 %fusion.26 = f32[8,64,2048]{2,1,0:T(8,128)} fusion(f32[8,64,2048]{2,1,0:T(8,128)} %get-tuple-element.150, s32[]{:T(128)S(6)} %copy.15, bf16[64,2048]{1,0:T(8,128)(2,1)S(1)} %get-tuple-element.161, bf16[2048,2176]{1,0:T(8,128)(2,1)} %get-tuple-element.160, s32[]{:T(128)S(6)} %select_n.19), kind=kOutput, calls=%fused_computation.4.clone.1 | convolution fusion | flops 537001984 | bytes 9699336 | tf_op jit(solution)/shard_map/while/body/eval_jaxpr/dot_general | solution.py:69
  143.5 7.7 %fusion.26 = f32[8,64,2048]{2,1,0:T(8,128)} fusion(f32[8,64,2048]{2,1,0:T(8,128)} %get-tuple-element.150, s32[]{:T(128)S(6)} %copy.15, bf16[64,2048]{1,0:T(8,128)(2,1)S(1)} %get-tuple-element.161, bf16[2048,2176]{1,0:T(8,128)(2,1)} %get-tuple-element.160, s32[]{:T(128)S(6)} %select_n.19), kind=kOutput, calls=%fused_computation.4.clone.1 | convolution fusion | flops 537001984 | bytes 9699336 | tf_op jit(solution)/shard_map/while/body/eval_jaxpr/dot_general | solution.py:69
  151.1 7.7 %fusion.26 = f32[8,64,2048]{2,1,0:T(8,128)} fusion(f32[8,64,2048]{2,1,0:T(8,128)} %get-tuple-element.150, s32[]{:T(128)S(6)} %copy.15, bf16[64,2048]{1,0:T(8,128)(2,1)S(1)} %get-tuple-element.161, bf16[2048,2176]{1,0:T(8,128)(2,1)} %get-tuple-element.160, s32[]{:T(128)S(6)} %select_n.19), kind=kOutput, calls=%fused_computation.4.clone.1 | convolution fusion | flops 537001984 | bytes 9699336 | tf_op jit(solution)/shard_map/while/body/eval_jaxpr/dot_general | solution.py:69
  158.8 7.7 %fusion.26 = f32[8,64,2048]{2,1,0:T(8,128)} fusion(f32[8,64,2048]{2,1,0:T(8,128)} %get-tuple-element.150, s32[]{:T(128)S(6)} %copy.15, bf16[64,2048]{1,0:T(8,128)(2,1)S(1)} %get-tuple-element.161, bf16[2048,2176]{1,0:T(8,128)(2,1)} %get-tuple-element.160, s32[]{:T(128)S(6)} %select_n.19), kind=kOutput, calls=%fused_computation.4.clone.1 | convolution fusion | flops 537001984 | bytes 9699336 | tf_op jit(solution)/shard_map/while/body/eval_jaxpr/dot_general | solution.py:69
  166.4 7.7 %fusion.26 = f32[8,64,2048]{2,1,0:T(8,128)} fusion(f32[8,64,2048]{2,1,0:T(8,128)} %get-tuple-element.150, s32[]{:T(128)S(6)} %copy.15, bf16[64,2048]{1,0:T(8,128)(2,1)S(1)} %get-tuple-element.161, bf16[2048,2176]{1,0:T(8,128)(2,1)} %get-tuple-element.160, s32[]{:T(128)S(6)} %select_n.19), kind=kOutput, calls=%fused_computation.4.clone.1 | convolution fusion | flops 537001984 | bytes 9699336 | tf_op jit(solution)/shard_map/while/body/eval_jaxpr/dot_general | solution.py:69
  174.1 7.7 %fusion.26 = f32[8,64,2048]{2,1,0:T(8,128)} fusion(f32[8,64,2048]{2,1,0:T(8,128)} %get-tuple-element.150, s32[]{:T(128)S(6)} %copy.15, bf16[64,2048]{1,0:T(8,128)(2,1)S(1)} %get-tuple-element.161, bf16[2048,2176]{1,0:T(8,128)(2,1)} %get-tuple-element.160, s32[]{:T(128)S(6)} %select_n.19), kind=kOutput, calls=%fused_computation.4.clone.1 | convolution fusion | flops 537001984 | bytes 9699336 | tf_op jit(solution)/shard_map/while/body/eval_jaxpr/dot_general | solution.py:69
  181.7 7.7 %fusion.26 = f32[8,64,2048]{2,1,0:T(8,128)} fusion(f32[8,64,2048]{2,1,0:T(8,128)} %get-tuple-element.150, s32[]{:T(128)S(6)} %copy.15, bf16[64,2048]{1,0:T(8,128)(2,1)S(1)} %get-tuple-element.161, bf16[2048,2176]{1,0:T(8,128)(2,1)} %get-tuple-element.160, s32[]{:T(128)S(6)} %select_n.19), kind=kOutput, calls=%fused_computation.4.clone.1 | convolution fusion | flops 537001984 | bytes 9699336 | tf_op jit(solution)/shard_map/while/body/eval_jaxpr/dot_general | solution.py:69
  189.4 4.9 %broadcast_multiply_fusion = f32[8,64,2048]{2,1,0:T(8,128)} fusion(f32[8,64,2048]{2,1,0:T(8,128)} %get-tuple-element.99, f32[2048]{0:T(1024)S(1)} %mul.38), kind=kLoop, calls=%fused_computation.7 | loop fusion | flops 1048576 | bytes 8396800 | tf_op jit(solution)/shard_map/mul | solution.py:79
  (2 shorter events, 0.1 us)
Async XLA Ops:
  6.5 111.3 %all-gather.2.cloned.1.call-start = ((), (), s32[]{:S(2)}) async-start(), calls=%async_computation.1 | async-start | bytes 8650752 | tf_op jit(solution)/shard_map/all_gather | solution.py:62
  7.4 5.3 %collective-permute-start = (f32[64,56]{1,0:T(8,128)S(1)}, f32[64,56]{1,0:T(8,128)S(1)}, u32[]{:S(2)}, u32[]{:S(2)}) collective-permute-start(f32[64,56]{1,0:T(8,128)S(1)} %slice.3), channel_id=1, source_target_pairs={{0,1},{1,2},{2,3},{3,4},{4,5},{5,6},{6,7},{7,8},{8,9},{9,10},{10,1... | collective-permute-start | bytes 43016 | tf_op jit(solution)/shard_map/ppermute | solution.py:20
  125.6 2.5 %copy-start = (bf16[64,2048]{1,0:T(8,128)(2,1)S(1)}, bf16[64,2048]{1,0:T(8,128)(2,1)}, u32[]{:S(2)}) copy-start(bf16[64,2048]{1,0:T(8,128)(2,1)} %fusion.13) | copy-start | bytes 786436
Sparse Core Ops, SparseCore 0:
  34.5 83.2 all-gather.1
